TPU v7x, 32 devices: a whole 2x2x4 slice. The times are simulated.
32 devices in a mesh: pix: 16 (over z, y, x), mode: 2 (over core).
Axes of the slice: x: 2, y: 2, z: 4, core: 2. Of those that a mesh axis runs over, the one named last changes fastest.
Arguments:
- frames: float32 [384, 49152], P('mode', 'pix'), may hold values from -40 to 40
- basis: float32 [2048, 49152], P('mode', 'pix'), may hold values from -0.078125 to 0.078125
- annulus: int32 [64], P('pix'), may hold values from 0 to 7, as said below
- truncation: int32 [8], replicated, may hold values from 256 to 2048
Outputs:
- residual: float32 [384, 49152], P('mode', 'pix')
Inputs may be any that keep to these rules, and one draw needn't show every extreme that they name: Every annulus holds one block or more; the blocks of an annulus may lie anywhere in the image.
All inputs are finite; a program needn't handle non-finite values.
Results may differ from a plain program's by a relative error of at most 0.0001.
Values sent between devices are 32-bit elements; how exact they have to be, the bound alone decides.
No kernel may reach another device: no remote copies, remote signals or barrier semaphores. Data moves between devices by JAX's collectives and lax.ppermute only.
A program may use at most 128 MiB of HBM per device.

v0:
```python
import jax
import jax.numpy as jnp
from jax import lax
from jax.sharding import PartitionSpec as P

NA = 8
K_CHUNKS = 2
HIGHEST_PRECISION = lax.Precision.HIGHEST
PRODUCT_PRECISION = lax.Precision.HIGH


def butterfly_sum(value, axes, size):
    step = 1
    while step < size:
        pairs = [(i, i ^ step) for i in range(size)]
        value = value + lax.ppermute(value, axes, pairs)
        step *= 2
    return value


def local(frames, basis, annulus, truncation):
    own_rows, pix_dev = frames.shape
    groups = lax.axis_size("mode")
    parts = lax.axis_size("pix")
    total_frames = own_rows * groups
    blocks = annulus.shape[0]
    block_len = pix_dev // blocks
    modes_dev = basis.shape[0]
    gathered = lax.all_gather(frames, "mode", axis=0, tiled=True)
    mode_index = lax.axis_index("mode")
    onehot = (annulus[:, None] == jnp.arange(NA, dtype=jnp.int32)[None, :]).astype(jnp.float32)
    own_block_sums = jnp.stack(
        [jnp.sum(frames[:, b * block_len : (b + 1) * block_len], axis=1) for b in range(blocks)],
        axis=0,
    )
    own_sums = jnp.einsum("ba,bf->af", onehot, own_block_sums, precision=HIGHEST_PRECISION)
    frame_slot = (mode_index * own_rows + jnp.arange(own_rows, dtype=jnp.int32))[
        :, None
    ] == jnp.arange(total_frames, dtype=jnp.int32)[None, :]
    local_sums = jnp.einsum(
        "af,fg->ag", own_sums, frame_slot.astype(jnp.float32), precision=HIGHEST_PRECISION
    )
    first_group = (mode_index == 0).astype(jnp.float32)
    local_counts = jnp.sum(onehot, axis=0) * (block_len * first_group)
    own_slot = (lax.axis_index("pix") * blocks + jnp.arange(blocks, dtype=jnp.int32))[
        :, None
    ] == jnp.arange(parts * blocks, dtype=jnp.int32)[None, :]
    local_table = (
        jnp.einsum("ba,bc->ac", onehot, own_slot.astype(jnp.float32), precision=HIGHEST_PRECISION)
        * first_group
    )
    packed = butterfly_sum(
        jnp.concatenate([local_sums, local_counts[:, None], local_table], axis=1),
        ("pix", "mode"),
        parts * groups,
    )
    annulus_totals = packed[:, :total_frames]
    pixel_counts = packed[:, total_frames]
    every_onehot = packed[:, total_frames + 1 :].T
    mode_ids = mode_index * modes_dev + jnp.arange(modes_dev, dtype=jnp.int32)
    retained = (mode_ids[None, :] < truncation[:, None]).astype(jnp.float32)
    annulus_means = annulus_totals / pixel_counts[:, None]
    block_means = jnp.einsum("ba,af->bf", onehot, annulus_means, precision=HIGHEST_PRECISION)
    chunk = modes_dev // K_CHUNKS
    same_annulus = jnp.einsum("ca,ba->cb", every_onehot, every_onehot, precision=HIGHEST_PRECISION)
    block_retained = jnp.einsum("ba,ak->bk", every_onehot, retained, precision=HIGHEST_PRECISION)
    rows_dev = total_frames // parts

    def piece_of(c, b):
        return lax.dynamic_slice(basis, (c * chunk, b * block_len), (chunk, block_len))

    def outbound(c):

        def body(b, per_block):
            mean = lax.dynamic_index_in_dim(block_means, b, 0, keepdims=False)
            centered = (
                lax.dynamic_slice_in_dim(gathered, b * block_len, block_len, 1) - mean[:, None]
            )
            product = jnp.dot(centered, piece_of(c, b).T, precision=PRODUCT_PRECISION)
            return lax.dynamic_update_index_in_dim(per_block, product, b, 0)

        per_block = lax.fori_loop(
            0, blocks, body, jnp.zeros((blocks, total_frames, chunk), jnp.float32)
        )
        return per_block.reshape(blocks, parts, rows_dev, chunk).transpose(1, 0, 2, 3)

    def inbound(c, arrived):
        summed = jnp.einsum(
            "cb,bfk->cfk",
            same_annulus,
            arrived.reshape(parts * blocks, rows_dev, chunk),
            precision=HIGHEST_PRECISION,
        )
        outgoing = summed * block_retained[:, None, c * chunk : (c + 1) * chunk]
        return outgoing.reshape(parts, blocks, rows_dev, chunk)

    def model_of(c, returned):
        picked = returned.transpose(1, 0, 2, 3).reshape(blocks, total_frames, chunk)

        def body(b, term):
            coefficients = lax.dynamic_index_in_dim(picked, b, 0, keepdims=False)
            product = jnp.dot(coefficients, piece_of(c, b), precision=PRODUCT_PRECISION)
            return lax.dynamic_update_slice_in_dim(term, product, b * block_len, 1)

        return lax.fori_loop(0, blocks, body, jnp.zeros((total_frames, pix_dev), jnp.float32))

    term = None
    pending = None
    for stage in range(K_CHUNKS + 1):
        sending = []
        if stage < K_CHUNKS:
            sending.append(outbound(stage))
        if pending is not None:
            sending.append(pending)
        received = lax.all_to_all(jnp.stack(sending, axis=1), "pix", 0, 0, tiled=True)
        slot = 0
        next_pending = None
        if stage < K_CHUNKS:
            next_pending = inbound(stage, received[:, 0])
            slot = 1
        if pending is not None:
            part = model_of(stage - 1, received[:, slot])
            term = part if term is None else term + part
        pending = next_pending
    model_rows = lax.psum_scatter(term, "mode", scatter_dimension=0, tiled=True)
    own_means = lax.dynamic_slice_in_dim(block_means, mode_index * own_rows, own_rows, 1)
    own_centered = jnp.concatenate(
        [
            frames[:, b * block_len : (b + 1) * block_len] - own_means[b][:, None]
            for b in range(blocks)
        ],
        axis=1,
    )
    return own_centered - model_rows


def solution(mesh):
    return jax.shard_map(
        local,
        mesh=mesh,
        in_specs=(P("mode", "pix"), P("mode", "pix"), P("pix"), P()),
        out_specs=P("mode", "pix"),
        check_vma=False,
    )
```

profile of v0, /device:TPU:0, one launch (start us, length us, event | category | flops | bytes accessed | tf_op | source)
XLA Modules:
  0.0 523.1 jit_solution(12102426613418549742)
XLA Ops:
  30.1 78.8 %while.53 = (s32[]{:T(128)}, f32[4,384,512]{2,0,1:T(4,128)}, f32[384,3072]{1,0:T(8,128)}, f32[4,384]{1,0:T(4,128)S(1)}, f32[1024,3072]{1,0:T(8,128)}, /*index=5*/s32[]{:T(128)}, s32[]{:T(128)}, s32[]{:T(128)}, s32[]{:T(128)}) while((s32[]{:T(128)}, f32[4,384,512]{2,0,1:T(4,128)}, f32[384,3072]{1,0:T(8,128)}, f32[4,384]{1,0:T(4,128)S(1)}, ...), condition=%wide.region_8.9_spmd, body=%wide.region_7.8_spmd.sunk | while | flops 906264576 | bytes 6690451 | solution.py:82
  33.8 16.0 %dynamic_update_slice.36 = f32[4,384,512]{2,0,1:T(4,128)} dynamic-update-slice(f32[4,384,512]{2,0,1:T(4,128)} %get-tuple-element.572, f32[1,384,512]{2,0,1:T(1,128)S(1)} %copy.56, s32[]{:T(128)} %get-tuple-element.571, s32[]{:T(128)} %constant.181.clone.1..sunk.1, s32[]{:T(128)} %constant.181.clone.1..sunk.1) | dynamic-update-slice | bytes 1572868 | tf_op jit(solution)/shard_map/while/body/eval_jaxpr/jit(dynamic_update_index_in_dim)/dynamic_update_slice | solution.py:80
  53.5 16.0 %dynamic_update_slice.36 = f32[4,384,512]{2,0,1:T(4,128)} dynamic-update-slice(f32[4,384,512]{2,0,1:T(4,128)} %get-tuple-element.572, f32[1,384,512]{2,0,1:T(1,128)S(1)} %copy.56, s32[]{:T(128)} %get-tuple-element.571, s32[]{:T(128)} %constant.181.clone.1..sunk.1, s32[]{:T(128)} %constant.181.clone.1..sunk.1) | dynamic-update-slice | bytes 1572868 | tf_op jit(solution)/shard_map/while/body/eval_jaxpr/jit(dynamic_update_index_in_dim)/dynamic_update_slice | solution.py:80
  73.2 16.0 %dynamic_update_slice.36 = f32[4,384,512]{2,0,1:T(4,128)} dynamic-update-slice(f32[4,384,512]{2,0,1:T(4,128)} %get-tuple-element.572, f32[1,384,512]{2,0,1:T(1,128)S(1)} %copy.56, s32[]{:T(128)} %get-tuple-element.571, s32[]{:T(128)} %constant.181.clone.1..sunk.1, s32[]{:T(128)} %constant.181.clone.1..sunk.1) | dynamic-update-slice | bytes 1572868 | tf_op jit(solution)/shard_map/while/body/eval_jaxpr/jit(dynamic_update_index_in_dim)/dynamic_update_slice | solution.py:80
  92.9 16.0 %dynamic_update_slice.36 = f32[4,384,512]{2,0,1:T(4,128)} dynamic-update-slice(f32[4,384,512]{2,0,1:T(4,128)} %get-tuple-element.572, f32[1,384,512]{2,0,1:T(1,128)S(1)} %copy.56, s32[]{:T(128)} %get-tuple-element.571, s32[]{:T(128)} %constant.181.clone.1..sunk.1, s32[]{:T(128)} %constant.181.clone.1..sunk.1) | dynamic-update-slice | bytes 1572868 | tf_op jit(solution)/shard_map/while/body/eval_jaxpr/jit(dynamic_update_index_in_dim)/dynamic_update_slice | solution.py:80
  108.9 7.4 %all-to-all-start = ((f32[16,1,4,24,512]{4,2,3,1,0:T(4,128)}), f32[16,1,4,24,512]{4,2,3,1,0:T(4,128)}, u32[]{:S(2)}, u32[]{:S(2)}) async-start(f32[16,1,4,24,512]{4,2,3,1,0:T(4,128)} %bitcast.64), calls=%async_computation | async-start | bytes 6291456 | tf_op jit(solution)/shard_map/all_to_all | solution.py:115
  119.3 78.9 %while.52 = (s32[]{:T(128)}, f32[4,384,512]{2,0,1:T(4,128)}, f32[384,3072]{1,0:T(8,128)}, f32[4,384]{1,0:T(4,128)S(1)}, f32[1024,3072]{1,0:T(8,128)}, /*index=5*/s32[]{:T(128)}, s32[]{:T(128)}, s32[]{:T(128)}, s32[]{:T(128)}) while((s32[]{:T(128)}, f32[4,384,512]{2,0,1:T(4,128)}, f32[384,3072]{1,0:T(8,128)}, f32[4,384]{1,0:T(4,128)S(1)}, ...), condition=%wide.region_6.7_spmd, body=%wide.region_5.6_spmd.sunk | while | flops 906264576 | bytes 6690451 | solution.py:82
  123.0 16.0 %dynamic_update_slice.35 = f32[4,384,512]{2,0,1:T(4,128)} dynamic-update-slice(f32[4,384,512]{2,0,1:T(4,128)} %get-tuple-element.545, f32[1,384,512]{2,0,1:T(1,128)S(1)} %copy.55, s32[]{:T(128)} %get-tuple-element.544, s32[]{:T(128)} %constant.181.clone.1..sunk, s32[]{:T(128)} %constant.181.clone.1..sunk) | dynamic-update-slice | bytes 1572868 | tf_op jit(solution)/shard_map/while/body/eval_jaxpr/jit(dynamic_update_index_in_dim)/dynamic_update_slice | solution.py:80
  142.7 16.0 %dynamic_update_slice.35 = f32[4,384,512]{2,0,1:T(4,128)} dynamic-update-slice(f32[4,384,512]{2,0,1:T(4,128)} %get-tuple-element.545, f32[1,384,512]{2,0,1:T(1,128)S(1)} %copy.55, s32[]{:T(128)} %get-tuple-element.544, s32[]{:T(128)} %constant.181.clone.1..sunk, s32[]{:T(128)} %constant.181.clone.1..sunk) | dynamic-update-slice | bytes 1572868 | tf_op jit(solution)/shard_map/while/body/eval_jaxpr/jit(dynamic_update_index_in_dim)/dynamic_update_slice | solution.py:80
  162.4 16.0 %dynamic_update_slice.35 = f32[4,384,512]{2,0,1:T(4,128)} dynamic-update-slice(f32[4,384,512]{2,0,1:T(4,128)} %get-tuple-element.545, f32[1,384,512]{2,0,1:T(1,128)S(1)} %copy.55, s32[]{:T(128)} %get-tuple-element.544, s32[]{:T(128)} %constant.181.clone.1..sunk, s32[]{:T(128)} %constant.181.clone.1..sunk) | dynamic-update-slice | bytes 1572868 | tf_op jit(solution)/shard_map/while/body/eval_jaxpr/jit(dynamic_update_index_in_dim)/dynamic_update_slice | solution.py:80
  182.1 16.0 %dynamic_update_slice.35 = f32[4,384,512]{2,0,1:T(4,128)} dynamic-update-slice(f32[4,384,512]{2,0,1:T(4,128)} %get-tuple-element.545, f32[1,384,512]{2,0,1:T(1,128)S(1)} %copy.55, s32[]{:T(128)} %get-tuple-element.544, s32[]{:T(128)} %constant.181.clone.1..sunk, s32[]{:T(128)} %constant.181.clone.1..sunk) | dynamic-update-slice | bytes 1572868 | tf_op jit(solution)/shard_map/while/body/eval_jaxpr/jit(dynamic_update_index_in_dim)/dynamic_update_slice | solution.py:80
  202.6 4.9 reshape_squeeze.6
  207.5 6.3 %broadcast_multiply_fusion.1 = f32[64,24,512]{2,0,1:T(8,128)} fusion(f32[64,512]{1,0:T(8,128)S(1)} %get-tuple-element.418, f32[64,64,1]{1,0,2:T(8,128)S(1)} %convolution_bitcast_fusion, f32[64,24,512]{2,0,1:T(8,128)} %reshape_squeeze.6), kind=kOutput, calls=%fused_computation.32 | convolution fusion | flops 604766208 | bytes 6438912 | tf_op jit(solution)/shard_map/cb,bfk->cfk/dot_general | solution.py:88
  213.9 4.8 stack_reshape.6
  218.7 4.6 pad_maximum_fusion
  223.3 143.2 %all_to_all.15 = f32[16,2,4,24,512]{4,2,3,1,0:T(4,128)S(1)} all-to-all(f32[16,2,4,24,512]{4,2,3,1,0:T(4,128)S(1)} %pad_maximum_fusion), channel_id=1, replica_groups=mesh['pix'=16,'mode'=2] {'pix'}, dimensions={0} | all-to-all | bytes 12582912 | tf_op jit(solution)/shard_map/all_to_all | solution.py:115
  372.3 4.9 reshape_squeeze.7
  377.2 6.4 %broadcast_multiply_fusion = f32[64,24,512]{2,0,1:T(8,128)} fusion(f32[64,512]{1,0:T(8,128)S(1)} %get-tuple-element.417, f32[64,64,1]{1,0,2:T(8,128)S(1)} %convolution_bitcast_fusion, f32[64,24,512]{2,0,1:T(8,128)} %reshape_squeeze.7), kind=kOutput, calls=%fused_computation.31 | convolution fusion | flops 604766208 | bytes 6438912 | tf_op jit(solution)/shard_map/cb,bfk->cfk/dot_general | solution.py:88
  383.6 4.8 stack_reshape.7
  400.2 24.9 %while.54 = (s32[]{:T(128)}, f32[384,3072]{1,0:T(8,128)}, f32[4,384,512]{2,0,1:T(4,128)}, f32[1024,3072]{1,0:T(8,128)}, s32[]{:T(128)}, /*index=5*/s32[]{:T(128)}, s32[]{:T(128)}, s32[]{:T(128)}) while((s32[]{:T(128)}, f32[384,3072]{1,0:T(8,128)}, f32[4,384,512]{2,0,1:T(4,128)}, f32[1024,3072]{1,0:T(8,128)}, s32[]{:T(128)}, ...), condition=%wide.region_10.11_spmd, body=%wide.region_9.10_spmd.sunk | while | flops 905969664 | bytes 5112967 | solution.py:105
  425.1 31.7 %all-to-all-done.2 = f32[16,1,4,24,512]{4,2,3,1,0:T(4,128)} async-done(((f32[16,1,4,24,512]{4,2,3,1,0:T(4,128)}), f32[16,1,4,24,512]{4,2,3,1,0:T(4,128)}, u32[]{:S(2)}, u32[]{:S(2)}) %all-to-all-start.2) | async-done | bytes 3145760 | tf_op jit(solution)/shard_map/all_to_all | solution.py:115
  459.5 24.9 %while.55 = (s32[]{:T(128)}, f32[384,3072]{1,0:T(8,128)}, f32[4,384,512]{2,0,1:T(4,128)}, f32[1024,3072]{1,0:T(8,128)}, s32[]{:T(128)}, /*index=5*/s32[]{:T(128)}, s32[]{:T(128)}, s32[]{:T(128)}) while((s32[]{:T(128)}, f32[384,3072]{1,0:T(8,128)}, f32[4,384,512]{2,0,1:T(4,128)}, f32[1024,3072]{1,0:T(8,128)}, s32[]{:T(128)}, ...), condition=%wide.region_12.13_spmd, body=%wide.region_11.12_spmd.sunk | while | flops 905969664 | bytes 5112967 | solution.py:105
  484.5 6.9 %add.186 = f32[384,3072]{1,0:T(8,128)} add(f32[384,3072]{1,0:T(8,128)} %get-tuple-element.353, f32[384,3072]{1,0:T(8,128)} %get-tuple-element.354) | non-fusion elementwise | flops 1179648 | bytes 14155776 | tf_op jit(solution)/shard_map/add | solution.py:123
  492.7 19.9 %reduce-scatter.2.cloned.1.call-done = f32[192,3072]{1,0:T(8,128)} async-done(((f32[384,3072]{1,0:T(8,128)}), f32[192,3072]{1,0:T(8,128)}) %reduce-scatter.2.cloned.1.call-update) | async-done | bytes 2359312 | tf_op jit(solution)/shard_map/reduce_scatter | solution.py:125
  (95 shorter events, 135.6 us)
Async XLA Ops:
  6.5 1.7 copy-start
  6.5 1.9 copy-start.2
  6.5 21.4 %all-gather.2.cloned.1.call-start = ((), (), s32[]{:S(2)}) async-start(), calls=%async_computation.4 | async-start | bytes 7077888 | tf_op jit(solution)/shard_map/all_gather | solution.py:29
  9.3 1.3 collective-permute-start
  10.7 4.5 collective-permute-start.1
  15.2 3.8 collective-permute-start.2
  19.0 3.8 collective-permute-start.3
  22.8 4.8 collective-permute-start.4
  108.9 7.8 %copy-start.1 = (s32[8]{0:T(128)S(1)}, s32[8]{0:T(128)}, u32[]{:S(2)}) copy-start(s32[8]{0:T(128)} %param.15) | copy-start | bytes 100
  108.9 89.2 %all-to-all-start = ((f32[16,1,4,24,512]{4,2,3,1,0:T(4,128)}), f32[16,1,4,24,512]{4,2,3,1,0:T(4,128)}, u32[]{:S(2)}, u32[]{:S(2)}) async-start(f32[16,1,4,24,512]{4,2,3,1,0:T(4,128)} %bitcast.64), calls=%async_computation | async-start | bytes 6291456 | tf_op jit(solution)/shard_map/all_to_all | solution.py:115
  392.8 64.0 %all-to-all-start.2 = ((f32[16,1,4,24,512]{4,2,3,1,0:T(4,128)}), f32[16,1,4,24,512]{4,2,3,1,0:T(4,128)}, u32[]{:S(2)}, u32[]{:S(2)}) async-start(f32[16,1,4,24,512]{4,2,3,1,0:T(4,128)} %copy.31), calls=%async_computation.2 | async-start | bytes 6291456 | tf_op jit(solution)/shard_map/all_to_all | solution.py:115
  397.3 115.3 %reduce-scatter.2.cloned.1.call-start = ((), (), s32[]{:S(2)}) async-start(), calls=%async_computation.5 | async-start | bytes 7077888 | tf_op jit(solution)/shard_map/reduce_scatter | solution.py:125
Sparse Core Ops, SparseCore 0:
  8.9 17.1 all-gather.1
  491.5 21.0 reduce-scatter.1
where the time goes:
time: 528 us; the launch traced here: 523 us
  local copies, waits for them, and re-layouts  199 us (38%)
  blocking collectives  143 us (27%)
  matrix products  66.8 us (13%)
  waiting for transfers between devices  60.1 us (11%)
  starting transfers between devices  22.4 us (4%)
  other arithmetic  17.6 us (3%)
  between operations  13.5 us (3%)
    all_to_all x1, blocking collectives, local(): lax.all_to_all(jnp.stack(sending, axis=1), 'pix', 0, 0, tiled=True)  143 us
    dynamic_update_slice x16, local copies, waits for them, and re-layouts, body(): return lax.dynamic_update_index_in_dim(per_block, product, b, 0)  134 us
    all_to_all x2, waiting for transfers between devices, local(): lax.all_to_all(jnp.stack(sending, axis=1), 'pix', 0, 0, tiled=True)  31.7 us
    dot_general x8, matrix products, body(): product = jnp.dot(coefficients, piece_of(c, b), precision=PRODUCT_PRECISION)  29.3 us
    dot_general x8, matrix products, body(): product = jnp.dot(centered, piece_of(c, b).T, precision=PRODUCT_PRECISION)  23.1 us
    dynamic_slice x8, local copies, waits for them, and re-layouts, body(): coefficients = lax.dynamic_index_in_dim(picked, b, 0, keepdims=False)  20.5 us
    reduce_scatter x1, waiting for transfers between devices, local(): model_rows = lax.psum_scatter(term, 'mode', scatter_dimension=0, tiled=True)  19.9 us
    another operation x3, local copies, waits for them, and re-layouts, local(): jnp.stack(sending, axis=1)  14.1 us
  transfers between devices with their start and end apart: 9, of which 7 were waited for; matrix products, arithmetic and copies ran while one was open for 22% of the time, Pallas kernels for 0%

commit v1 on v0

--- a/solution.py
+++ b/solution.py
@@ -112,7 +112,27 @@
             sending.append(outbound(stage))
         if pending is not None:
             sending.append(pending)
-        received = lax.all_to_all(jnp.stack(sending, axis=1), "pix", 0, 0, tiled=True)
+
+        def open_screen_in(v0):
+            front, d_next = (lax.axis_size("pix"), lax.axis_index("pix"))
+            raw_out = v0.shape[0] // front
+            lower = list(v0.shape)
+            lower[0] = raw_out
+            piece_now = lower[0]
+            lower[0] = piece_now * front
+            part_next = jnp.zeros(lower, v0.dtype)
+            for idx in range(front):
+                long_array = lax.dynamic_slice_in_dim(v0, (d_next ^ idx) * raw_out, raw_out, axis=0)
+                if idx:
+                    long_array = lax.ppermute(
+                        long_array, "pix", [(k, k ^ idx) for k in range(front)]
+                    )
+                part_next = lax.dynamic_update_slice_in_dim(
+                    part_next, long_array, (d_next ^ idx) * piece_now, axis=0
+                )
+            return part_next
+
+        received = open_screen_in(jnp.stack(sending, axis=1))
         slot = 0
         next_pending = None
         if stage < K_CHUNKS:

time: 528 us -> 483 us (0.915)
  blocking collectives: 143 us -> 0 us
  starting transfers between devices: 22.4 us -> 150 us
  local copies, waits for them, and re-layouts: 199 us -> 73.2 us
  waiting for transfers between devices: 60.1 us -> 162 us
    all_to_all x1 -> x0, blocking collectives: 143 us -> none  [local(): lax.all_to_all(jnp.stack(sending, axis=1), 'pix', 0, 0, tiled=True)]
    ppermute x0 -> x45, starting transfers between devices: none -> 139 us  [open_screen_in(): lax.ppermute(long_array, 'pix', [(k, k ^ idx) for k in range(front)])]
    ppermute x0 -> x45, waiting for transfers between devices: none -> 137 us  [open_screen_in(): lax.ppermute(long_array, 'pix', [(k, k ^ idx) for k in range(front)])]
    dynamic_update_slice x16 -> x47, local copies, waits for them, and re-layouts: 134 us -> 25.5 us  [open_screen_in(): lax.dynamic_update_slice_in_dim(part_next, long_array, (d_next ^ idx) * p...]
    all_to_all x2 -> x0, waiting for transfers between devices: 31.7 us -> none  [local(): lax.all_to_all(jnp.stack(sending, axis=1), 'pix', 0, 0, tiled=True)]
    dynamic_slice x8 -> x2, local copies, waits for them, and re-layouts: 20.5 us -> 3.57 us  [open_screen_in(): lax.dynamic_slice_in_dim(v0, (d_next ^ idx) * raw_out, raw_out, axis=0)]
    all_to_all x2 -> x0, starting transfers between devices: 11.9 us -> none  [local(): lax.all_to_all(jnp.stack(sending, axis=1), 'pix', 0, 0, tiled=True)]
    another operation x7, local copies, waits for them, and re-layouts: 23.9 us -> 16.8 us  [the longest x3 14.1 us: local(): jnp.stack(sending, axis=1)]
  transfers between devices with their start and end apart: 9 -> 52, of which waited for: 7 -> 21; matrix products, arithmetic and copies ran while one was open for 22% -> 15% of each run, Pallas kernels for 0% -> 0%
where the time goes in v1:
time: 483 us; the launch traced here: 481 us
  waiting for transfers between devices  162 us (34%)
  starting transfers between devices  150 us (31%)
  local copies, waits for them, and re-layouts  73.2 us (15%)
  matrix products  65 us (13%)
  other arithmetic  17.1 us (4%)
  between operations  14.1 us (3%)
    ppermute x45, starting transfers between devices, open_screen_in(): lax.ppermute(long_array, 'pix', [(k, k ^ idx) for k in range(front)])  139 us
    ppermute x45, waiting for transfers between devices, open_screen_in(): lax.ppermute(long_array, 'pix', [(k, k ^ idx) for k in range(front)])  137 us
    dot_general x8, matrix products, body(): product = jnp.dot(coefficients, piece_of(c, b), precision=PRODUCT_PRECISION)  29.3 us
    dynamic_update_slice x47, local copies, waits for them, and re-layouts, open_screen_in(): lax.dynamic_update_slice_in_dim(part_next, long_array, (d_next ^ idx) * p...  25.5 us
    dot_general x8, matrix products, body(): product = jnp.dot(centered, piece_of(c, b).T, precision=PRODUCT_PRECISION)  23.1 us
    reduce_scatter x1, waiting for transfers between devices, local(): model_rows = lax.psum_scatter(term, 'mode', scatter_dimension=0, tiled=True)  17 us
    dot_general x2, matrix products, inbound(): jnp.einsum('cb,bfk->cfk', same_annulus, arrived.reshape(parts * blocks, r...  10.8 us
    ppermute x5, starting transfers between devices, butterfly_sum(): value = value + lax.ppermute(value, axes, pairs)  10.5 us
  transfers between devices with their start and end apart: 52, of which 21 were waited for; matrix products, arithmetic and copies ran while one was open for 15% of the time, Pallas kernels for 0%

profile of v1, /device:TPU:0, one launch (start us, length us, event | category | flops | bytes accessed | tf_op | source)
XLA Modules:
  0.0 481.2 jit_solution(9580562444360894323)
XLA Ops:
  29.7 11.8 %while.53 = (s32[]{:T(128)}, f32[4,384,512]{2,1,0:T(8,128)S(1)}, f32[384,3072]{1,0:T(8,128)}, f32[4,384]{1,0:T(4,128)S(1)}, f32[1024,3072]{1,0:T(8,128)}, /*index=5*/s32[]{:T(128)}, s32[]{:T(128)}, s32[]{:T(128)}, s32[]{:T(128)}) while((s32[]{:T(128)}, f32[4,384,512]{2,1,0:T(8,128)S(1)}, f32[384,3072]{1,0:T(8,128)}, f32[4,384]{1,0:T(4,128)S(1)}, ...), condition=%wide.region_8.9_spmd, body=%wide.region_7.8_spmd.sunk | while | flops 906264576 | bytes 3545743 | solution.py:82
  50.3 11.8 %while.52 = (s32[]{:T(128)}, f32[4,384,512]{2,1,0:T(8,128)S(1)}, f32[384,3072]{1,0:T(8,128)}, f32[4,384]{1,0:T(4,128)S(1)}, f32[1024,3072]{1,0:T(8,128)}, /*index=5*/s32[]{:T(128)}, s32[]{:T(128)}, s32[]{:T(128)}, s32[]{:T(128)}) while((s32[]{:T(128)}, f32[4,384,512]{2,1,0:T(8,128)S(1)}, f32[384,3072]{1,0:T(8,128)}, f32[4,384]{1,0:T(4,128)S(1)}, ...), condition=%wide.region_6.7_spmd, body=%wide.region_5.6_spmd.sunk | while | flops 906264576 | bytes 3545743 | solution.py:82
  95.7 11.1 %collective-permute-done.12 = f32[1,1,4,24,512]{4,3,2,1,0:T(8,128)S(1)} collective-permute-done((f32[1,1,4,24,512]{4,3,2,1,0:T(8,128)S(1)}, f32[1,1,4,24,512]{4,3,2,1,0:T(8,128)S(1)}, u32[]{:S(2)}, u32[]{:S(2)}) %collective-permute-start.12) | collective-permute-done | bytes 196640 | tf_op jit(solution)/shard_map/ppermute | solution.py:127
  111.3 5.2 %collective-permute-done.13 = f32[1,1,4,24,512]{4,3,2,1,0:T(8,128)S(1)} collective-permute-done((f32[1,1,4,24,512]{4,3,2,1,0:T(8,128)S(1)}, f32[1,1,4,24,512]{4,3,2,1,0:T(8,128)S(1)}, u32[]{:S(2)}, u32[]{:S(2)}) %collective-permute-start.13) | collective-permute-done | bytes 196640 | tf_op jit(solution)/shard_map/ppermute | solution.py:127
  116.5 8.0 %collective-permute-start.18 = (f32[1,1,4,24,512]{4,3,2,1,0:T(8,128)S(1)}, f32[1,1,4,24,512]{4,3,2,1,0:T(8,128)S(1)}, u32[]{:S(2)}, u32[]{:S(2)}) collective-permute-start(f32[1,1,4,24,512]{4,3,2,1,0:T(8,128)S(1)} %copy-done.13), channel_id=1, source_target_pairs={{0,28},{2,30},{4,24},{6,26},{8,20},{10,22},{12,16},{14,18},{16,12}... | collective-permute-start | bytes 589832 | tf_op jit(solution)/shard_map/ppermute | solution.py:127
  135.5 5.0 %reshape_squeeze.6 = f32[64,24,512]{2,0,1:T(8,128)} reshape(f32[16,1,4,24,512]{4,2,0,3,1:T(4,128)} %copy_dynamic-update-slice_fusion.15) | data formatting | bytes 6291456 | tf_op jit(solution)/shard_map/reshape;squeeze | solution.py:91
  140.5 6.3 %convolution_multiply_fusion.1 = f32[64,24,512]{2,0,1:T(8,128)} fusion(f32[64,64,1]{1,0,2:T(8,128)S(1)} %convolution_bitcast_fusion, f32[64,24,512]{2,0,1:T(8,128)} %reshape_squeeze.6, f32[64,512]{1,0:T(8,128)S(1)} %copy-done.8), kind=kOutput, calls=%fused_computation.68 | convolution fusion | flops 604766208 | bytes 6438912 | tf_op jit(solution)/shard_map/cb,bfk->cfk/dot_general | solution.py:88
  162.3 12.4 %collective-permute-start.23 = (f32[1,2,4,24,512]{4,2,0,3,1:T(4,128)}, f32[1,2,4,24,512]{4,2,0,3,1:T(4,128)S(1)}, u32[]{:S(2)}, u32[]{:S(2)}) collective-permute-start(f32[1,2,4,24,512]{4,2,0,3,1:T(4,128)} %get-tuple-element.402), channel_id=1, source_target_pairs={{0,8},{2,10},{4,12},{6,14},{8,0},{10,2},{12,4},{14,6},{16,24},{18,... | collective-permute-start | bytes 1179656 | tf_op jit(solution)/shard_map/ppermute | solution.py:127
  177.2 8.5 %collective-permute-start.25 = (f32[1,2,4,24,512]{4,2,0,3,1:T(4,128)S(1)}, f32[1,2,4,24,512]{4,2,0,3,1:T(4,128)S(1)}, u32[]{:S(2)}, u32[]{:S(2)}) collective-permute-start(f32[1,2,4,24,512]{4,2,0,3,1:T(4,128)S(1)} %get-tuple-element.405), channel_id=1, source_target_pairs={{0,12},{2,14},{4,8},{6,10},{8,4},{10,6},{12,0},{14,2},{16,28},{18,... | collective-permute-start | bytes 1179656 | tf_op jit(solution)/shard_map/ppermute | solution.py:127
  187.0 17.8 %collective-permute-start.27 = (f32[1,2,4,24,512]{4,2,0,3,1:T(4,128)S(1)}, f32[1,2,4,24,512]{4,2,0,3,1:T(4,128)S(1)}, u32[]{:S(2)}, u32[]{:S(2)}) collective-permute-start(f32[1,2,4,24,512]{4,2,0,3,1:T(4,128)S(1)} %get-tuple-element.407), channel_id=1, source_target_pairs={{0,16},{2,18},{4,20},{6,22},{8,24},{10,26},{12,28},{14,30},{16,0},... | collective-permute-start | bytes 1179656 | tf_op jit(solution)/shard_map/ppermute | solution.py:127
  207.9 7.3 %collective-permute-done.25 = f32[1,2,4,24,512]{4,2,0,3,1:T(4,128)S(1)} collective-permute-done((f32[1,2,4,24,512]{4,2,0,3,1:T(4,128)S(1)}, f32[1,2,4,24,512]{4,2,0,3,1:T(4,128)S(1)}, u32[]{:S(2)}, u32[]{:S(2)}) %collective-permute-start.25) | collective-permute-done | bytes 393248 | tf_op jit(solution)/shard_map/ppermute | solution.py:127
  223.0 41.8 %collective-permute-done.27 = f32[1,2,4,24,512]{4,2,0,3,1:T(4,128)S(1)} collective-permute-done((f32[1,2,4,24,512]{4,2,0,3,1:T(4,128)S(1)}, f32[1,2,4,24,512]{4,2,0,3,1:T(4,128)S(1)}, u32[]{:S(2)}, u32[]{:S(2)}) %collective-permute-start.27) | collective-permute-done | bytes 393248 | tf_op jit(solution)/shard_map/ppermute | solution.py:127
  265.4 13.3 %collective-permute-done.28 = f32[1,2,4,24,512]{4,2,0,3,1:T(4,128)S(1)} collective-permute-done((f32[1,2,4,24,512]{4,2,0,3,1:T(4,128)S(1)}, f32[1,2,4,24,512]{4,2,0,3,1:T(4,128)S(1)}, u32[]{:S(2)}, u32[]{:S(2)}) %collective-permute-start.28) | collective-permute-done | bytes 393248 | tf_op jit(solution)/shard_map/ppermute | solution.py:127
  278.8 15.2 %collective-permute-done.29 = f32[1,2,4,24,512]{4,2,0,3,1:T(4,128)S(1)} collective-permute-done((f32[1,2,4,24,512]{4,2,0,3,1:T(4,128)S(1)}, f32[1,2,4,24,512]{4,2,0,3,1:T(4,128)S(1)}, u32[]{:S(2)}, u32[]{:S(2)}) %collective-permute-start.29) | collective-permute-done | bytes 393248 | tf_op jit(solution)/shard_map/ppermute | solution.py:127
  294.1 6.4 %collective-permute-done.30 = f32[1,2,4,24,512]{4,2,0,3,1:T(4,128)S(1)} collective-permute-done((f32[1,2,4,24,512]{4,2,0,3,1:T(4,128)S(1)}, f32[1,2,4,24,512]{4,2,0,3,1:T(4,128)S(1)}, u32[]{:S(2)}, u32[]{:S(2)}) %collective-permute-start.30) | collective-permute-done | bytes 393248 | tf_op jit(solution)/shard_map/ppermute | solution.py:127
  300.8 4.8 collective-permute-done.34
  326.6 22.1 %collective-permute-start.38 = (f32[1,1,4,24,512]{4,2,0,3,1:T(4,128)}, f32[1,1,4,24,512]{4,2,0,3,1:T(4,128)}, u32[]{:S(2)}, u32[]{:S(2)}) collective-permute-start(f32[1,1,4,24,512]{4,2,0,3,1:T(4,128)} %get-tuple-element.424), channel_id=1, source_target_pairs={{0,8},{2,10},{4,12},{6,14},{8,0},{10,2},{12,4},{14,6},{16,24},{18,... | collective-permute-start | bytes 589832 | tf_op jit(solution)/shard_map/ppermute | solution.py:127
  354.4 14.7 %while.54 = (s32[]{:T(128)}, f32[384,3072]{1,0:T(8,128)}, f32[4,384,512]{2,1,0:T(8,128)S(1)}, f32[1024,3072]{1,0:T(8,128)}, s32[]{:T(128)}, /*index=5*/s32[]{:T(128)}, s32[]{:T(128)}, s32[]{:T(128)}) while((s32[]{:T(128)}, f32[384,3072]{1,0:T(8,128)}, f32[4,384,512]{2,1,0:T(8,128)S(1)}, f32[1024,3072]{1,0:T(8,128)}, s32[]{:T(128)}, ...), condition=%wide.region_10.11_spmd, body=%wide.region_9.10_spmd.sunk | while | flops 905969664 | bytes 3540611 | solution.py:105
  388.8 12.4 %collective-permute-done.42 = f32[1,1,4,24,512]{4,2,0,3,1:T(4,128)S(1)} collective-permute-done((f32[1,1,4,24,512]{4,2,0,3,1:T(4,128)S(1)}, f32[1,1,4,24,512]{4,2,0,3,1:T(4,128)S(1)}, u32[]{:S(2)}, u32[]{:S(2)}) %collective-permute-start.42) | collective-permute-done | bytes 196640 | tf_op jit(solution)/shard_map/ppermute | solution.py:127
  408.6 8.3 %collective-permute-done.44 = f32[1,1,4,24,512]{4,2,0,3,1:T(4,128)S(1)} collective-permute-done((f32[1,1,4,24,512]{4,2,0,3,1:T(4,128)S(1)}, f32[1,1,4,24,512]{4,2,0,3,1:T(4,128)S(1)}, u32[]{:S(2)}, u32[]{:S(2)}) %collective-permute-start.44) | collective-permute-done | bytes 196640 | tf_op jit(solution)/shard_map/ppermute | solution.py:127
  421.4 4.9 %collective-permute-done.49 = f32[1,1,4,24,512]{4,2,0,3,1:T(4,128)S(1)} collective-permute-done((f32[1,1,4,24,512]{4,2,0,3,1:T(4,128)S(1)}, f32[1,1,4,24,512]{4,2,0,3,1:T(4,128)S(1)}, u32[]{:S(2)}, u32[]{:S(2)}) %collective-permute-start.49) | collective-permute-done | bytes 196640 | tf_op jit(solution)/shard_map/ppermute | solution.py:127
  429.1 14.6 %while.55 = (s32[]{:T(128)}, f32[384,3072]{1,0:T(8,128)}, f32[4,384,512]{2,1,0:T(8,128)S(1)}, f32[1024,3072]{1,0:T(8,128)}, s32[]{:T(128)}, /*index=5*/s32[]{:T(128)}, s32[]{:T(128)}, s32[]{:T(128)}) while((s32[]{:T(128)}, f32[384,3072]{1,0:T(8,128)}, f32[4,384,512]{2,1,0:T(8,128)S(1)}, f32[1024,3072]{1,0:T(8,128)}, s32[]{:T(128)}, ...), condition=%wide.region_12.13_spmd, body=%wide.region_11.12_spmd.sunk | while | flops 905969664 | bytes 3540611 | solution.py:105
  443.8 7.0 %add.330 = f32[384,3072]{1,0:T(8,128)} add(f32[384,3072]{1,0:T(8,128)} %get-tuple-element.353, f32[384,3072]{1,0:T(8,128)} %get-tuple-element.354) | non-fusion elementwise | flops 1179648 | bytes 14155776 | tf_op jit(solution)/shard_map/add | solution.py:143
  453.7 17.0 %reduce-scatter.2.cloned.1.call-done = f32[192,3072]{1,0:T(8,128)} async-done(((f32[384,3072]{1,0:T(8,128)}), f32[192,3072]{1,0:T(8,128)}) %reduce-scatter.2.cloned.1.call-update) | async-done | bytes 2359312 | tf_op jit(solution)/shard_map/reduce_scatter | solution.py:145
  (265 shorter events, 232.1 us)
Async XLA Ops:
  7.3 463.4 %reduce-scatter.2.cloned.1.call-start = ((), (), s32[]{:S(2)}) async-start(), calls=%async_computation.2 | async-start | bytes 7077888 | tf_op jit(solution)/shard_map/reduce_scatter | solution.py:145
  46.6 35.1 %collective-permute-start.8 = (f32[1,1,4,24,512]{4,3,2,1,0:T(8,128)}, f32[1,1,4,24,512]{4,3,2,1,0:T(8,128)}, u32[]{:S(2)}, u32[]{:S(2)}) collective-permute-start(f32[1,1,4,24,512]{4,3,2,1,0:T(8,128)} %get-tuple-element.440), channel_id=1, source_target_pairs={{0,8},{2,10},{4,12},{6,14},{8,0},{10,2},{12,4},{14,6},{16,24},{18,... | collective-permute-start | bytes 589832 | tf_op jit(solution)/shard_map/ppermute | solution.py:127
  48.5 36.3 %collective-permute-start.9 = (f32[1,1,4,24,512]{4,3,2,1,0:T(8,128)}, f32[1,1,4,24,512]{4,3,2,1,0:T(8,128)}, u32[]{:S(2)}, u32[]{:S(2)}) collective-permute-start(f32[1,1,4,24,512]{4,3,2,1,0:T(8,128)} %get-tuple-element.439), channel_id=1, source_target_pairs={{0,10},{2,8},{4,14},{6,12},{8,2},{10,0},{12,6},{14,4},{16,26},{18,... | collective-permute-start | bytes 589832 | tf_op jit(solution)/shard_map/ppermute | solution.py:127
  81.8 34.7 %collective-permute-start.13 = (f32[1,1,4,24,512]{4,3,2,1,0:T(8,128)S(1)}, f32[1,1,4,24,512]{4,3,2,1,0:T(8,128)S(1)}, u32[]{:S(2)}, u32[]{:S(2)}) collective-permute-start(f32[1,1,4,24,512]{4,3,2,1,0:T(8,128)S(1)} %copy-done.22), channel_id=1, source_target_pairs={{0,18},{2,16},{4,22},{6,20},{8,26},{10,24},{12,30},{14,28},{16,2},... | collective-permute-start | bytes 589832 | tf_op jit(solution)/shard_map/ppermute | solution.py:127
  84.8 40.5 %collective-permute-start.14 = (f32[1,1,4,24,512]{4,3,2,1,0:T(8,128)S(1)}, f32[1,1,4,24,512]{4,3,2,1,0:T(8,128)S(1)}, u32[]{:S(2)}, u32[]{:S(2)}) collective-permute-start(f32[1,1,4,24,512]{4,3,2,1,0:T(8,128)S(1)} %copy-done.20), channel_id=1, source_target_pairs={{0,20},{2,22},{4,16},{6,18},{8,28},{10,30},{12,24},{14,26},{16,4},... | collective-permute-start | bytes 589832 | tf_op jit(solution)/shard_map/ppermute | solution.py:127
  90.2 41.1 %collective-permute-start.15 = (f32[1,1,4,24,512]{4,3,2,1,0:T(8,128)S(1)}, f32[1,1,4,24,512]{4,3,2,1,0:T(8,128)S(1)}, u32[]{:S(2)}, u32[]{:S(2)}) collective-permute-start(f32[1,1,4,24,512]{4,3,2,1,0:T(8,128)S(1)} %copy-done.18), channel_id=1, source_target_pairs={{0,22},{2,20},{4,18},{6,16},{8,30},{10,28},{12,26},{14,24},{16,6},... | collective-permute-start | bytes 589832 | tf_op jit(solution)/shard_map/ppermute | solution.py:127
  91.0 41.1 %collective-permute-start.16 = (f32[1,1,4,24,512]{4,3,2,1,0:T(8,128)S(1)}, f32[1,1,4,24,512]{4,3,2,1,0:T(8,128)S(1)}, u32[]{:S(2)}, u32[]{:S(2)}) collective-permute-start(f32[1,1,4,24,512]{4,3,2,1,0:T(8,128)S(1)} %copy-done.17), channel_id=1, source_target_pairs={{0,24},{2,26},{4,28},{6,30},{8,16},{10,18},{12,20},{14,22},{16,8},... | collective-permute-start | bytes 589832 | tf_op jit(solution)/shard_map/ppermute | solution.py:127
  162.3 42.5 %collective-permute-start.23 = (f32[1,2,4,24,512]{4,2,0,3,1:T(4,128)}, f32[1,2,4,24,512]{4,2,0,3,1:T(4,128)S(1)}, u32[]{:S(2)}, u32[]{:S(2)}) collective-permute-start(f32[1,2,4,24,512]{4,2,0,3,1:T(4,128)} %get-tuple-element.402), channel_id=1, source_target_pairs={{0,8},{2,10},{4,12},{6,14},{8,0},{10,2},{12,4},{14,6},{16,24},{18,... | collective-permute-start | bytes 1179656 | tf_op jit(solution)/shard_map/ppermute | solution.py:127
  177.2 38.0 %collective-permute-start.25 = (f32[1,2,4,24,512]{4,2,0,3,1:T(4,128)S(1)}, f32[1,2,4,24,512]{4,2,0,3,1:T(4,128)S(1)}, u32[]{:S(2)}, u32[]{:S(2)}) collective-permute-start(f32[1,2,4,24,512]{4,2,0,3,1:T(4,128)S(1)} %get-tuple-element.405), channel_id=1, source_target_pairs={{0,12},{2,14},{4,8},{6,10},{8,4},{10,6},{12,0},{14,2},{16,28},{18,... | collective-permute-start | bytes 1179656 | tf_op jit(solution)/shard_map/ppermute | solution.py:127
  186.8 33.9 %collective-permute-start.26 = (f32[1,2,4,24,512]{4,2,0,3,1:T(4,128)S(1)}, f32[1,2,4,24,512]{4,2,0,3,1:T(4,128)S(1)}, u32[]{:S(2)}, u32[]{:S(2)}) collective-permute-start(f32[1,2,4,24,512]{4,2,0,3,1:T(4,128)S(1)} %get-tuple-element.406), channel_id=1, source_target_pairs={{0,14},{2,12},{4,10},{6,8},{8,6},{10,4},{12,2},{14,0},{16,30},{18,... | collective-permute-start | bytes 1179656 | tf_op jit(solution)/shard_map/ppermute | solution.py:127
  187.0 77.8 %collective-permute-start.27 = (f32[1,2,4,24,512]{4,2,0,3,1:T(4,128)S(1)}, f32[1,2,4,24,512]{4,2,0,3,1:T(4,128)S(1)}, u32[]{:S(2)}, u32[]{:S(2)}) collective-permute-start(f32[1,2,4,24,512]{4,2,0,3,1:T(4,128)S(1)} %get-tuple-element.407), channel_id=1, source_target_pairs={{0,16},{2,18},{4,20},{6,22},{8,24},{10,26},{12,28},{14,30},{16,0},... | collective-permute-start | bytes 1179656 | tf_op jit(solution)/shard_map/ppermute | solution.py:127
  204.8 73.9 %collective-permute-start.28 = (f32[1,2,4,24,512]{4,2,0,3,1:T(4,128)S(1)}, f32[1,2,4,24,512]{4,2,0,3,1:T(4,128)S(1)}, u32[]{:S(2)}, u32[]{:S(2)}) collective-permute-start(f32[1,2,4,24,512]{4,2,0,3,1:T(4,128)S(1)} %get-tuple-element.408), channel_id=1, source_target_pairs={{0,18},{2,16},{4,22},{6,20},{8,26},{10,24},{12,30},{14,28},{16,2},... | collective-permute-start | bytes 1179656 | tf_op jit(solution)/shard_map/ppermute | solution.py:127
  205.7 88.3 %collective-permute-start.29 = (f32[1,2,4,24,512]{4,2,0,3,1:T(4,128)S(1)}, f32[1,2,4,24,512]{4,2,0,3,1:T(4,128)S(1)}, u32[]{:S(2)}, u32[]{:S(2)}) collective-permute-start(f32[1,2,4,24,512]{4,2,0,3,1:T(4,128)S(1)} %get-tuple-element.410), channel_id=1, source_target_pairs={{0,20},{2,22},{4,16},{6,18},{8,28},{10,30},{12,24},{14,26},{16,4},... | collective-permute-start | bytes 1179656 | tf_op jit(solution)/shard_map/ppermute | solution.py:127
  215.2 85.3 %collective-permute-start.30 = (f32[1,2,4,24,512]{4,2,0,3,1:T(4,128)S(1)}, f32[1,2,4,24,512]{4,2,0,3,1:T(4,128)S(1)}, u32[]{:S(2)}, u32[]{:S(2)}) collective-permute-start(f32[1,2,4,24,512]{4,2,0,3,1:T(4,128)S(1)} %get-tuple-element.411), channel_id=1, source_target_pairs={{0,22},{2,20},{4,18},{6,16},{8,30},{10,28},{12,26},{14,24},{16,6},... | collective-permute-start | bytes 1179656 | tf_op jit(solution)/shard_map/ppermute | solution.py:127
  220.7 79.8 %collective-permute-start.31 = (f32[1,2,4,24,512]{4,2,0,3,1:T(4,128)S(1)}, f32[1,2,4,24,512]{4,2,0,3,1:T(4,128)S(1)}, u32[]{:S(2)}, u32[]{:S(2)}) collective-permute-start(f32[1,2,4,24,512]{4,2,0,3,1:T(4,128)S(1)} %get-tuple-element.412), channel_id=1, source_target_pairs={{0,24},{2,26},{4,28},{6,30},{8,16},{10,18},{12,20},{14,22},{16,8},... | collective-permute-start | bytes 1179656 | tf_op jit(solution)/shard_map/ppermute | solution.py:127
  264.8 35.9 %collective-permute-start.32 = (f32[1,2,4,24,512]{4,2,0,3,1:T(4,128)S(1)}, f32[1,2,4,24,512]{4,2,0,3,1:T(4,128)S(1)}, u32[]{:S(2)}, u32[]{:S(2)}) collective-permute-start(f32[1,2,4,24,512]{4,2,0,3,1:T(4,128)S(1)} %get-tuple-element.409), channel_id=1, source_target_pairs={{0,26},{2,24},{4,30},{6,28},{8,18},{10,16},{12,22},{14,20},{16,10}... | collective-permute-start | bytes 1179656 | tf_op jit(solution)/shard_map/ppermute | solution.py:127
  322.2 47.4 %collective-permute-start.35 = (f32[1,1,4,24,512]{4,2,0,3,1:T(4,128)}, f32[1,1,4,24,512]{4,2,0,3,1:T(4,128)}, u32[]{:S(2)}, u32[]{:S(2)}) collective-permute-start(f32[1,1,4,24,512]{4,2,0,3,1:T(4,128)} %get-tuple-element.427), channel_id=1, source_target_pairs={{0,2},{2,0},{4,6},{6,4},{8,10},{10,8},{12,14},{14,12},{16,18},{18,... | collective-permute-start | bytes 589832 | tf_op jit(solution)/shard_map/ppermute | solution.py:127
  325.1 47.4 %collective-permute-start.36 = (f32[1,1,4,24,512]{4,2,0,3,1:T(4,128)}, f32[1,1,4,24,512]{4,2,0,3,1:T(4,128)}, u32[]{:S(2)}, u32[]{:S(2)}) collective-permute-start(f32[1,1,4,24,512]{4,2,0,3,1:T(4,128)} %get-tuple-element.426), channel_id=1, source_target_pairs={{0,4},{2,6},{4,0},{6,2},{8,12},{10,14},{12,8},{14,10},{16,20},{18,... | collective-permute-start | bytes 589832 | tf_op jit(solution)/shard_map/ppermute | solution.py:127
  325.1 49.9 %collective-permute-start.37 = (f32[1,1,4,24,512]{4,2,0,3,1:T(4,128)}, f32[1,1,4,24,512]{4,2,0,3,1:T(4,128)}, u32[]{:S(2)}, u32[]{:S(2)}) collective-permute-start(f32[1,1,4,24,512]{4,2,0,3,1:T(4,128)} %get-tuple-element.425), channel_id=1, source_target_pairs={{0,6},{2,4},{4,2},{6,0},{8,14},{10,12},{12,10},{14,8},{16,22},{18,... | collective-permute-start | bytes 589832 | tf_op jit(solution)/shard_map/ppermute | solution.py:127
  326.6 52.0 %collective-permute-start.38 = (f32[1,1,4,24,512]{4,2,0,3,1:T(4,128)}, f32[1,1,4,24,512]{4,2,0,3,1:T(4,128)}, u32[]{:S(2)}, u32[]{:S(2)}) collective-permute-start(f32[1,1,4,24,512]{4,2,0,3,1:T(4,128)} %get-tuple-element.424), channel_id=1, source_target_pairs={{0,8},{2,10},{4,12},{6,14},{8,0},{10,2},{12,4},{14,6},{16,24},{18,... | collective-permute-start | bytes 589832 | tf_op jit(solution)/shard_map/ppermute | solution.py:127
  348.7 32.3 %collective-permute-start.39 = (f32[1,1,4,24,512]{4,2,0,3,1:T(4,128)}, f32[1,1,4,24,512]{4,2,0,3,1:T(4,128)}, u32[]{:S(2)}, u32[]{:S(2)}) collective-permute-start(f32[1,1,4,24,512]{4,2,0,3,1:T(4,128)} %get-tuple-element.423), channel_id=1, source_target_pairs={{0,10},{2,8},{4,14},{6,12},{8,2},{10,0},{12,6},{14,4},{16,26},{18,... | collective-permute-start | bytes 589832 | tf_op jit(solution)/shard_map/ppermute | solution.py:127
  381.0 35.9 %collective-permute-start.44 = (f32[1,1,4,24,512]{4,2,0,3,1:T(4,128)S(1)}, f32[1,1,4,24,512]{4,2,0,3,1:T(4,128)S(1)}, u32[]{:S(2)}, u32[]{:S(2)}) collective-permute-start(f32[1,1,4,24,512]{4,2,0,3,1:T(4,128)S(1)} %copy-done.19), channel_id=1, source_target_pairs={{0,20},{2,22},{4,16},{6,18},{8,28},{10,30},{12,24},{14,26},{16,4},... | collective-permute-start | bytes 589832 | tf_op jit(solution)/shard_map/ppermute | solution.py:127
  384.7 36.3 %collective-permute-start.45 = (f32[1,1,4,24,512]{4,2,0,3,1:T(4,128)S(1)}, f32[1,1,4,24,512]{4,2,0,3,1:T(4,128)S(1)}, u32[]{:S(2)}, u32[]{:S(2)}) collective-permute-start(f32[1,1,4,24,512]{4,2,0,3,1:T(4,128)S(1)} %copy-done.16), channel_id=1, source_target_pairs={{0,22},{2,20},{4,18},{6,16},{8,30},{10,28},{12,26},{14,24},{16,6},... | collective-permute-start | bytes 589832 | tf_op jit(solution)/shard_map/ppermute | solution.py:127
  386.3 34.8 %collective-permute-start.46 = (f32[1,1,4,24,512]{4,2,0,3,1:T(4,128)S(1)}, f32[1,1,4,24,512]{4,2,0,3,1:T(4,128)S(1)}, u32[]{:S(2)}, u32[]{:S(2)}) collective-permute-start(f32[1,1,4,24,512]{4,2,0,3,1:T(4,128)S(1)} %copy-done.14), channel_id=1, source_target_pairs={{0,24},{2,26},{4,28},{6,30},{8,16},{10,18},{12,20},{14,22},{16,8},... | collective-permute-start | bytes 589832 | tf_op jit(solution)/shard_map/ppermute | solution.py:127
  (59 other events, 1081.2 us)
Sparse Core Ops, SparseCore 0:
  8.9 17.1 all-gather.1
  450.9 19.7 reduce-scatter.1
